TPU v7x, 32 devices: a whole 2x2x4 slice. The times are simulated.
32 devices in a mesh: groups: 1, gx: 32 (over z, y, x, core).
Axes of the slice: x: 2, y: 2, z: 4, core: 2. Of those that a mesh axis runs over, the one named last changes fastest.
Arguments:
- solid_state: float32 [9, 2, 1, 256, 4, 128], P(None, None, 'groups', 'gx'), may hold values from -6 to 6
- water_state: float32 [4, 2, 1, 128, 12, 256], P(None, None, 'groups', 'gx'), may hold values from -6 to 6
- lame_lambda: float32 [256, 4, 128], P('gx'), may hold values from 0.4 to 1.2
- shear_mu: float32 [256, 4, 128], P('gx'), may hold values from 0.1 to 0.5
- solid_buoy: float32 [256, 4, 128], P('gx'), may hold values from 0.4 to 1
- water_kappa: float32 [128, 12, 256], P('gx'), may hold values from 0.5 to 1
- water_buoy: float32 [128, 12, 256], P('gx'), may hold values from 0.6 to 1.2
- seafloor: int32 [128, 256], P('gx'), may hold values from 6 to 12
- source_cell: int32 [1], P('groups'), may hold values from 0 to 196607
- wavelet: float32 [4, 1], P(None, 'groups'), may hold values from -48 to 48
- receiver_column: int32 [128], replicated, may hold values from 0 to 32767
- observed: float32 [4, 1, 128], P(None, 'groups'), may hold values from -6 to 6
Outputs:
- grad_lambda: float32 [256, 4, 128], P('gx', 'groups')
- grad_mu: float32 [256, 4, 128], P('gx', 'groups')
- grad_kappa: float32 [128, 12, 256], P('gx', 'groups')
- residuals: float32 [4, 1, 128], P(None, 'groups')
Inputs may be any that keep to these rules, and one draw needn't show every extreme that they name: Every column holds water from z = 0 to z = seafloor - 1 and rock below it. source_cell is (z * 128 + y) * 256 + x of a water cell with z below 6. receiver_column is y * 256 + x; two nodes may share a column.
All inputs are finite; a program needn't handle non-finite values.
Results may differ from a plain program's by a relative error of at most 0.00014.
Values sent between devices are 32-bit elements; how exact they have to be, the bound alone decides.
No kernel may reach another device: no remote copies, remote signals or barrier semaphores. Data moves between devices by JAX's collectives and lax.ppermute only.
A program may use at most 64 MiB of HBM per device.

v0:
```python
import jax
import jax.numpy as jnp
from jax import lax
from jax.sharding import PartitionSpec as P

COEFF = (1225.0 / 1024.0, -245.0 / 3072.0, 49.0 / 5120.0, -5.0 / 7168.0)
TIME_STEP = 0.2


def with_halo(array, sides, width):
    for axis, dim in sides:
        devices, length = (lax.axis_size(axis), array.shape[dim])
        up = [(i, (i + 1) % devices) for i in range(devices - 1)]
        down = [(j, i) for i, j in up]
        last = lax.slice_in_dim(array, length - width, length, axis=dim)
        first = lax.slice_in_dim(array, 0, width, axis=dim)
        before = lax.ppermute(last, axis, up)
        after = lax.ppermute(first, axis, down)
        array = jnp.concatenate([before, array, after], axis=dim)
    return array


def stencil(padded, axis, forward):
    length = padded.shape[axis] - 8
    summed = None
    for offset in range(1, 5):
        if forward:
            front_at, back_at = (4 + offset, 5 - offset)
        else:
            front_at, back_at = (3 + offset, 4 - offset)
        front = lax.slice_in_dim(padded, front_at, front_at + length, axis=axis)
        back = lax.slice_in_dim(padded, back_at, back_at + length, axis=axis)
        addend = COEFF[offset - 1] * (front - back)
        summed = addend if summed is None else summed + addend
    return summed


def padded_zero(field, axis):
    widths = [(0, 0)] * field.ndim
    widths[axis] = (4, 4)
    return jnp.pad(field, widths)


def derive(field, axis, forward):
    return stencil(padded_zero(field, axis), axis, forward)


def on_device(
    solid_state,
    water_state,
    lame_lambda,
    shear_mu,
    solid_buoy,
    water_kappa,
    water_buoy,
    seafloor,
    source_cell,
    wavelet,
    receiver_column,
    observed,
):
    parts = lax.axis_size("gx")
    place = lax.axis_index("gx")
    width_x = solid_state.shape[3]
    total_y = solid_state.shape[5]
    total_x = width_x * parts
    shots = solid_state.shape[2]
    shard_axis = 2
    anchor_y = place * water_state.shape[3]
    anchor_x = 0

    def water_halo(field):
        return with_halo(field, (("gx", 2),), 4)

    def water_derive(field, axis, forward):
        if axis == shard_axis:
            return stencil(water_halo(field), axis, forward)
        return derive(field, axis, forward)

    def solid_halo(stacked):
        return with_halo(stacked, (("gx", 3),), 4)

    vel_x, vel_y, vel_z = (solid_state[0], solid_state[1], solid_state[2])
    sig_xx, sig_yy, sig_zz = (solid_state[3], solid_state[4], solid_state[5])
    sig_xy, sig_xz, sig_yz = (solid_state[6], solid_state[7], solid_state[8])
    pressure, flow_x, flow_y, flow_z = (
        water_state[0],
        water_state[1],
        water_state[2],
        water_state[3],
    )
    local_y = pressure.shape[2]
    depth_rows = pressure.shape[3]
    local_x = pressure.shape[4]
    depth_idx = lax.broadcasted_iota(jnp.int32, (1, depth_rows, 1), 1)
    floor_rows = seafloor[:, None, :]
    live = (depth_idx < floor_rows).astype(jnp.float32)
    bottom = (depth_idx == floor_rows - 1).astype(jnp.float32)
    above = (depth_idx < floor_rows - 1).astype(jnp.float32)
    rows_y = lax.broadcasted_iota(jnp.int32, (local_y, 1, 1), 0) + anchor_y
    cols_x = lax.broadcasted_iota(jnp.int32, (1, 1, local_x), 2) + anchor_x
    flat_cell = (depth_idx * total_y + rows_y) * total_x + cols_x
    source_hot = (flat_cell[None] == source_cell[:, None, None, None]).astype(jnp.float32)
    node_y = receiver_column // total_x
    node_x = receiver_column % total_x
    inside = (
        (node_y >= anchor_y)
        & (node_y < anchor_y + local_y)
        & (node_x >= anchor_x)
        & (node_x < anchor_x + local_x)
    )
    local_col = (node_y - anchor_y) * local_x + (node_x - anchor_x)
    column_iota = lax.broadcasted_iota(jnp.int32, (1, local_y * local_x), 1)
    node_hot = ((column_iota == local_col[:, None]) & inside[:, None]).astype(jnp.float32)
    grad_lambda = jnp.zeros(lame_lambda.shape, jnp.float32)
    grad_mu = jnp.zeros(lame_lambda.shape, jnp.float32)
    grad_kappa = jnp.zeros(water_kappa.shape, jnp.float32)
    misfits = []
    for step in range(wavelet.shape[0]):
        floor_pressure = jnp.sum(pressure * bottom, axis=3)
        stress_pad = solid_halo(jnp.stack([sig_xx, sig_xy, sig_xz]))
        vel_x = vel_x + TIME_STEP * solid_buoy * (
            stencil(stress_pad[0], 2, True) + derive(sig_xy, 4, False) + derive(sig_xz, 3, False)
        )
        vel_y = vel_y + TIME_STEP * solid_buoy * (
            stencil(stress_pad[1], 2, False) + derive(sig_yy, 4, True) + derive(sig_yz, 3, False)
        )
        vel_z = vel_z + TIME_STEP * solid_buoy * (
            stencil(stress_pad[2], 2, False) + derive(sig_yz, 4, False) + derive(sig_zz, 3, True)
        )
        floor_velocity = lax.all_to_all(
            jnp.transpose(vel_z[:, :, :, 0, :], (0, 1, 3, 2)),
            "gx",
            split_axis=2,
            concat_axis=3,
            tiled=True,
        )
        flow_x = (flow_x - TIME_STEP * water_buoy * water_derive(pressure, 4, True)) * live
        flow_y = (flow_y - TIME_STEP * water_buoy * water_derive(pressure, 2, True)) * live
        flow_z = (
            flow_z - TIME_STEP * water_buoy * derive(pressure, 3, True)
        ) * above + floor_velocity[:, :, :, None, :] * bottom
        velocity_pad = solid_halo(jnp.stack([vel_x, vel_y, vel_z]))
        strain_x = stencil(velocity_pad[0], 2, False)
        strain_y = derive(vel_y, 4, False)
        strain_z = derive(vel_z, 3, False)
        dilation = strain_x + strain_y + strain_z
        shear_xy = derive(vel_x, 4, True) + stencil(velocity_pad[1], 2, True)
        shear_xz = derive(vel_x, 3, True) + stencil(velocity_pad[2], 2, True)
        shear_yz = derive(vel_y, 3, True) + derive(vel_z, 4, True)
        lam_part = lame_lambda * dilation
        sig_xx = sig_xx + TIME_STEP * (lam_part + 2.0 * shear_mu * strain_x)
        sig_yy = sig_yy + TIME_STEP * (lam_part + 2.0 * shear_mu * strain_y)
        sig_zz = sig_zz + TIME_STEP * (lam_part + 2.0 * shear_mu * strain_z)
        sig_xy = sig_xy + TIME_STEP * shear_mu * shear_xy
        sig_xz = sig_xz + TIME_STEP * shear_mu * shear_xz
        sig_yz = sig_yz + TIME_STEP * shear_mu * shear_yz
        rock_pressure = jnp.transpose(
            lax.all_to_all(floor_pressure, "gx", split_axis=3, concat_axis=2, tiled=True),
            (0, 1, 3, 2),
        )
        sig_zz = sig_zz.at[:, :, :, 0, :].set(-rock_pressure)
        grad_lambda = grad_lambda + jnp.sum(dilation[0] * dilation[1], axis=0)
        normal_part = (
            strain_x[0] * strain_x[1] + strain_y[0] * strain_y[1] + strain_z[0] * strain_z[1]
        )
        shear_part = (
            shear_xy[0] * shear_xy[1] + shear_xz[0] * shear_xz[1] + shear_yz[0] * shear_yz[1]
        )
        grad_mu = grad_mu + jnp.sum(2.0 * normal_part + shear_part, axis=0)
        pressure = (
            pressure
            - TIME_STEP
            * water_kappa
            * (
                water_derive(flow_x, 4, False)
                + water_derive(flow_y, 2, False)
                + derive(flow_z, 3, False)
            )
        ) * live
        pressure = pressure.at[0].add(wavelet[step][:, None, None, None] * source_hot)
        surface = jnp.sum(pressure * bottom, axis=3)
        partial_record = jnp.einsum(
            "sc,rc->sr",
            surface[0].reshape(shots, local_y * local_x),
            node_hot,
            precision=lax.Precision.HIGHEST,
        )
        recorded = lax.psum(partial_record, "gx")
        misfit = recorded - observed[step]
        scaled = misfit * lax.rsqrt(jnp.mean(misfit * misfit, axis=1, keepdims=True) + 1e-06)
        inject = jnp.dot(
            scaled, node_hot, precision=lax.Precision.HIGHEST, preferred_element_type=jnp.float32
        ).reshape(shots, local_y, local_x)
        pressure = pressure.at[1].add(inject[:, :, None, :] * bottom)
        grad_kappa = grad_kappa + jnp.sum(pressure[0] * pressure[1], axis=0)
        misfits.append(misfit)
    return (grad_lambda, grad_mu, grad_kappa, jnp.stack(misfits))


def solution(mesh):
    placed = (
        P(None, None, "groups", "gx", None, None),
        P(None, None, "groups", "gx", None, None),
        P("gx", None, None),
        P("gx", None, None),
        P("gx", None, None),
        P("gx", None, None),
        P("gx", None, None),
        P("gx", None),
        P("groups"),
        P(None, "groups"),
        P(),
        P(None, "groups", None),
    )
    return jax.shard_map(
        on_device,
        mesh=mesh,
        in_specs=placed,
        out_specs=(
            P("gx", "groups", None),
            P("gx", "groups", None),
            P("gx", "groups", None),
            P(None, "groups", None),
        ),
        check_vma=False,
    )
```

profile of v0, /device:TPU:0, one launch (start us, length us, event | category | flops | bytes accessed | tf_op | source)
XLA Modules:
  0.0 367.0 jit_solution(11349562170741559003)
XLA Ops:
  2.9 3.0 collective-permute-start.11
  6.8 1.3 collective-permute-start.1
  8.1 5.1 %collective-permute-start = (f32[3,2,1,4,4,128]{5,4,3,2,1,0:T(4,128)S(1)}, f32[3,2,1,4,4,128]{5,4,3,2,1,0:T(4,128)S(1)}, u32[]{:S(2)}, u32[]{:S(2)}) collective-permute-start(f32[3,2,1,4,4,128]{5,4,3,2,1,0:T(4,128)S(1)} %get-tuple-element.248), channel_id=1, source_target_pairs={{0,1},{1,2},{2,3},{3,4},{4,5},{5,6},{6,7},{7,8},{8,9},{9,10},{10,1... | collective-permute-start | bytes 147464 | tf_op jit(solution)/shard_map/ppermute | solution.py:17
  19.5 9.7 %all-to-all-start.1 = ((f32[2,1,128,8]{3,0,1,2:T(2,128)}), f32[2,1,128,8]{3,0,1,2:T(2,128)S(1)}, u32[]{:S(2)}, u32[]{:S(2)}) async-start(f32[2,1,128,8]{3,0,1,2:T(2,128)} %copy.963), calls=%async_computation.1 | async-start | bytes 262144 | tf_op jit(solution)/shard_map/all_to_all | solution.py:131
  29.7 1.4 collective-permute-start.3
  31.2 3.0 collective-permute-start.2
  34.2 3.3 all-to-all-done.1
  39.1 1.3 collective-permute-start.5
  40.4 3.0 collective-permute-start.4
  43.9 3.4 collective-permute-start.12
  47.3 1.3 collective-permute-start.13
  49.1 1.4 collective-permute-done.13
  52.6 12.4 %all-to-all-start = ((f32[2,1,4,256]{2,0,1,3:T(2,128)}), f32[2,1,4,256]{2,0,1,3:T(2,128)S(1)}, u32[]{:S(2)}, u32[]{:S(2)}) async-start(f32[2,1,4,256]{2,0,1,3:T(2,128)} %copy.948), calls=%async_computation | async-start | bytes 524288 | tf_op jit(solution)/shard_map/all_to_all | solution.py:159
  65.5 40.5 %psum.28 = f32[1,128]{1,0:T(1,128)S(1)} all-reduce(f32[1,128]{1,0:T(1,128)S(1)} %fusion.7), channel_id=1, replica_groups=mesh['groups'=1,'gx'=32] {'gx'}, use_global_device_ids=true, to_apply=%region_2.3 | all-reduce | flops 128 | bytes 1024 | tf_op jit(solution)/shard_map/psum | solution.py:189
  107.8 1.3 collective-permute-start.18
  109.1 3.0 collective-permute-start.19
  113.6 6.2 %all-to-all-start.3 = ((f32[2,1,128,8]{3,0,1,2:T(2,128)}), f32[2,1,128,8]{3,0,1,2:T(2,128)S(1)}, u32[]{:S(2)}, u32[]{:S(2)}) async-start(f32[2,1,128,8]{3,0,1,2:T(2,128)} %copy.978), calls=%async_computation.3 | async-start | bytes 262144 | tf_op jit(solution)/shard_map/all_to_all | solution.py:131
  119.9 1.3 collective-permute-start.7
  121.2 3.0 collective-permute-start.6
  124.2 3.8 %all-to-all-done.3 = f32[2,1,128,8]{3,0,1,2:T(2,128)S(1)} async-done(((f32[2,1,128,8]{3,0,1,2:T(2,128)}), f32[2,1,128,8]{3,0,1,2:T(2,128)S(1)}, u32[]{:S(2)}, u32[]{:S(2)}) %all-to-all-start.3) | async-done | bytes 8224 | tf_op jit(solution)/shard_map/all_to_all | solution.py:131
  129.1 1.3 collective-permute-start.9
  130.4 3.0 collective-permute-start.8
  133.9 3.4 collective-permute-start.20
  137.3 1.3 collective-permute-start.21
  139.1 1.4 collective-permute-done.21
  142.7 11.9 %all-to-all-start.2 = ((f32[2,1,4,256]{2,0,1,3:T(2,128)}), f32[2,1,4,256]{2,0,1,3:T(2,128)S(1)}, u32[]{:S(2)}, u32[]{:S(2)}) async-start(f32[2,1,4,256]{2,0,1,3:T(2,128)} %copy.966), calls=%async_computation.2 | async-start | bytes 524288 | tf_op jit(solution)/shard_map/all_to_all | solution.py:159
  155.0 40.5 %psum.29 = f32[1,128]{1,0:T(1,128)S(1)} all-reduce(f32[1,128]{1,0:T(1,128)S(1)} %fusion.5), channel_id=1, replica_groups=mesh['groups'=1,'gx'=32] {'gx'}, use_global_device_ids=true, to_apply=%region_6.7 | all-reduce | flops 128 | bytes 1024 | tf_op jit(solution)/shard_map/psum | solution.py:189
  198.6 3.0 collective-permute-start.25
  203.1 6.2 %all-to-all-start.5 = ((f32[2,1,128,8]{3,0,1,2:T(2,128)}), f32[2,1,128,8]{3,0,1,2:T(2,128)S(1)}, u32[]{:S(2)}, u32[]{:S(2)}) async-start(f32[2,1,128,8]{3,0,1,2:T(2,128)} %copy.989), calls=%async_computation.5 | async-start | bytes 262144 | tf_op jit(solution)/shard_map/all_to_all | solution.py:131
  210.7 3.0 collective-permute-start.14
  213.7 3.8 %all-to-all-done.5 = f32[2,1,128,8]{3,0,1,2:T(2,128)S(1)} async-done(((f32[2,1,128,8]{3,0,1,2:T(2,128)}), f32[2,1,128,8]{3,0,1,2:T(2,128)S(1)}, u32[]{:S(2)}, u32[]{:S(2)}) %all-to-all-start.5) | async-done | bytes 8224 | tf_op jit(solution)/shard_map/all_to_all | solution.py:131
  219.9 3.0 collective-permute-start.16
  223.4 3.4 collective-permute-start.26
  226.8 1.3 collective-permute-start.27
  228.6 1.4 collective-permute-done.27
  232.2 11.9 %all-to-all-start.4 = ((f32[2,1,4,256]{2,0,1,3:T(2,128)}), f32[2,1,4,256]{2,0,1,3:T(2,128)S(1)}, u32[]{:S(2)}, u32[]{:S(2)}) async-start(f32[2,1,4,256]{2,0,1,3:T(2,128)} %copy.981), calls=%async_computation.4 | async-start | bytes 524288 | tf_op jit(solution)/shard_map/all_to_all | solution.py:159
  244.5 40.5 %psum.30 = f32[1,128]{1,0:T(1,128)S(1)} all-reduce(f32[1,128]{1,0:T(1,128)S(1)} %fusion.3), channel_id=1, replica_groups=mesh['groups'=1,'gx'=32] {'gx'}, use_global_device_ids=true, to_apply=%region_10.11 | all-reduce | flops 128 | bytes 1024 | tf_op jit(solution)/shard_map/psum | solution.py:189
  286.8 1.3 collective-permute-start.28
  288.1 3.0 collective-permute-start.29
  292.6 6.2 %all-to-all-start.6 = ((f32[2,1,128,8]{3,0,1,2:T(2,128)}), f32[2,1,128,8]{3,0,1,2:T(2,128)S(1)}, u32[]{:S(2)}, u32[]{:S(2)}) async-start(f32[2,1,128,8]{3,0,1,2:T(2,128)} %copy.992), calls=%async_computation.6 | async-start | bytes 262144 | tf_op jit(solution)/shard_map/all_to_all | solution.py:131
  298.9 1.3 collective-permute-start.23
  300.2 3.0 collective-permute-start.22
  303.2 3.8 %all-to-all-done.6 = f32[2,1,128,8]{3,0,1,2:T(2,128)S(1)} async-done(((f32[2,1,128,8]{3,0,1,2:T(2,128)}), f32[2,1,128,8]{3,0,1,2:T(2,128)S(1)}, u32[]{:S(2)}, u32[]{:S(2)}) %all-to-all-start.6) | async-done | bytes 8224 | tf_op jit(solution)/shard_map/all_to_all | solution.py:131
  309.1 2.1 collective-permute-start.30
  311.2 1.3 collective-permute-start.31
  313.2 1.9 collective-permute-done.31
  316.8 46.5 %psum.31 = f32[1,128]{1,0:T(1,128)S(1)} all-reduce(f32[1,128]{1,0:T(1,128)S(1)} %fusion.1), channel_id=1, replica_groups=mesh['groups'=1,'gx'=32] {'gx'}, use_global_device_ids=true, to_apply=%region_13.14 | all-reduce | flops 128 | bytes 1024 | tf_op jit(solution)/shard_map/psum | solution.py:189
  365.1 1.4 fusion.372
  (226 shorter events, 40.5 us)
Async XLA Ops:
  0.6 6.1 %copy-start = (f32[9,2,1,8,4,128]{5,4,3,2,1,0:T(4,128)S(1)}, f32[9,2,1,8,4,128]{5,4,3,2,1,0:T(4,128)}, u32[]{:S(2)}) copy-start(f32[9,2,1,8,4,128]{5,4,3,2,1,0:T(4,128)} %param.34) | copy-start | bytes 884740
  1.6 41.8 %collective-permute-start.10 = (f32[2,1,4,12,256]{4,2,3,1,0:T(4,128)S(1)}, f32[2,1,4,12,256]{4,2,3,1,0:T(4,128)S(1)}, u32[]{:S(2)}, u32[]{:S(2)}) collective-permute-start(f32[2,1,4,12,256]{4,2,3,1,0:T(4,128)S(1)} %slice_bitcast_fusion.3), channel_id=1, source_target_pairs={{1,0},{2,1},{3,2},{4,3},{5,4},{6,5},{7,6},{8,7},{9,8},{10,9},{11,1... | collective-permute-start | bytes 294920 | tf_op jit(solution)/shard_map/ppermute | solution.py:18
  2.9 40.5 %collective-permute-start.11 = (f32[2,1,4,12,256]{4,2,3,1,0:T(4,128)S(1)}, f32[2,1,4,12,256]{4,2,3,1,0:T(4,128)S(1)}, u32[]{:S(2)}, u32[]{:S(2)}) collective-permute-start(f32[2,1,4,12,256]{4,2,3,1,0:T(4,128)S(1)} %slice_bitcast_fusion.3), channel_id=1, source_target_pairs={{0,1},{1,2},{2,3},{3,4},{4,5},{5,6},{6,7},{7,8},{8,9},{9,10},{10,1... | collective-permute-start | bytes 294920 | tf_op jit(solution)/shard_map/ppermute | solution.py:17
  6.8 6.4 %copy-start.7 = (s32[4,256]{1,0:T(4,128)S(1)}, s32[4,256]{1,0:T(4,128)}, u32[]{:S(2)}) copy-start(s32[4,256]{1,0:T(4,128)} %param.41) | copy-start | bytes 12292
  6.8 11.5 %collective-permute-start.1 = (f32[3,2,1,4,4,128]{5,4,3,2,1,0:T(4,128)S(1)}, f32[3,2,1,4,4,128]{5,4,3,2,1,0:T(4,128)S(1)}, u32[]{:S(2)}, u32[]{:S(2)}) collective-permute-start(f32[3,2,1,4,4,128]{5,4,3,2,1,0:T(4,128)S(1)} %get-tuple-element.249), channel_id=1, source_target_pairs={{1,0},{2,1},{3,2},{4,3},{5,4},{6,5},{7,6},{8,7},{9,8},{10,9},{11,1... | collective-permute-start | bytes 147464 | tf_op jit(solution)/shard_map/ppermute | solution.py:18
  8.1 10.3 %collective-permute-start = (f32[3,2,1,4,4,128]{5,4,3,2,1,0:T(4,128)S(1)}, f32[3,2,1,4,4,128]{5,4,3,2,1,0:T(4,128)S(1)}, u32[]{:S(2)}, u32[]{:S(2)}) collective-permute-start(f32[3,2,1,4,4,128]{5,4,3,2,1,0:T(4,128)S(1)} %get-tuple-element.248), channel_id=1, source_target_pairs={{0,1},{1,2},{2,3},{3,4},{4,5},{5,6},{6,7},{7,8},{8,9},{9,10},{10,1... | collective-permute-start | bytes 147464 | tf_op jit(solution)/shard_map/ppermute | solution.py:17
  13.3 0.7 copy-start.6
  14.0 0.7 copy-start.5
  14.7 0.8 copy-start.3
  15.5 0.8 copy-start.4
  19.5 18.0 %all-to-all-start.1 = ((f32[2,1,128,8]{3,0,1,2:T(2,128)}), f32[2,1,128,8]{3,0,1,2:T(2,128)S(1)}, u32[]{:S(2)}, u32[]{:S(2)}) async-start(f32[2,1,128,8]{3,0,1,2:T(2,128)} %copy.963), calls=%async_computation.1 | async-start | bytes 262144 | tf_op jit(solution)/shard_map/all_to_all | solution.py:131
  29.7 8.0 %copy-start.1 = (f32[4,2,1,4,12,256]{5,3,4,2,1,0:T(4,128)S(1)}, f32[4,2,1,4,12,256]{5,3,4,2,1,0:T(4,128)}, u32[]{:S(2)}) copy-start(f32[4,2,1,4,12,256]{5,3,4,2,1,0:T(4,128)} %param.35) | copy-start | bytes 1179652
  29.7 8.0 %collective-permute-start.3 = (f32[3,2,1,4,4,128]{5,4,3,2,1,0:T(4,128)S(1)}, f32[3,2,1,4,4,128]{5,4,3,2,1,0:T(4,128)S(1)}, u32[]{:S(2)}, u32[]{:S(2)}) collective-permute-start(f32[3,2,1,4,4,128]{5,4,3,2,1,0:T(4,128)S(1)} %get-tuple-element.247), channel_id=1, source_target_pairs={{1,0},{2,1},{3,2},{4,3},{5,4},{6,5},{7,6},{8,7},{9,8},{10,9},{11,1... | collective-permute-start | bytes 147464 | tf_op jit(solution)/shard_map/ppermute | solution.py:18
  31.2 6.6 %collective-permute-start.2 = (f32[3,2,1,4,4,128]{5,4,3,2,1,0:T(4,128)S(1)}, f32[3,2,1,4,4,128]{5,4,3,2,1,0:T(4,128)S(1)}, u32[]{:S(2)}, u32[]{:S(2)}) collective-permute-start(f32[3,2,1,4,4,128]{5,4,3,2,1,0:T(4,128)S(1)} %get-tuple-element.246), channel_id=1, source_target_pairs={{0,1},{1,2},{2,3},{3,4},{4,5},{5,6},{6,7},{7,8},{8,9},{9,10},{10,1... | collective-permute-start | bytes 147464 | tf_op jit(solution)/shard_map/ppermute | solution.py:17
  37.9 0.7 copy-start.2
  39.1 9.5 %collective-permute-start.5 = (f32[3,2,1,4,4,128]{5,4,3,2,1,0:T(4,128)S(1)}, f32[3,2,1,4,4,128]{5,4,3,2,1,0:T(4,128)S(1)}, u32[]{:S(2)}, u32[]{:S(2)}) collective-permute-start(f32[3,2,1,4,4,128]{5,4,3,2,1,0:T(4,128)S(1)} %get-tuple-element.245), channel_id=1, source_target_pairs={{1,0},{2,1},{3,2},{4,3},{5,4},{6,5},{7,6},{8,7},{9,8},{10,9},{11,1... | collective-permute-start | bytes 147464 | tf_op jit(solution)/shard_map/ppermute | solution.py:18
  40.4 8.2 %collective-permute-start.4 = (f32[3,2,1,4,4,128]{5,4,3,2,1,0:T(4,128)S(1)}, f32[3,2,1,4,4,128]{5,4,3,2,1,0:T(4,128)S(1)}, u32[]{:S(2)}, u32[]{:S(2)}) collective-permute-start(f32[3,2,1,4,4,128]{5,4,3,2,1,0:T(4,128)S(1)} %get-tuple-element.244), channel_id=1, source_target_pairs={{0,1},{1,2},{2,3},{3,4},{4,5},{5,6},{6,7},{7,8},{8,9},{9,10},{10,1... | collective-permute-start | bytes 147464 | tf_op jit(solution)/shard_map/ppermute | solution.py:17
  43.9 5.2 %collective-permute-start.12 = (f32[2,1,4,12,256]{4,2,3,1,0:T(4,128)S(1)}, f32[2,1,4,12,256]{4,2,3,1,0:T(4,128)S(1)}, u32[]{:S(2)}, u32[]{:S(2)}) collective-permute-start(f32[2,1,4,12,256]{4,2,3,1,0:T(4,128)S(1)} %get-tuple-element.190), channel_id=1, source_target_pairs={{0,1},{1,2},{2,3},{3,4},{4,5},{5,6},{6,7},{7,8},{8,9},{9,10},{10,1... | collective-permute-start | bytes 294920 | tf_op jit(solution)/shard_map/ppermute | solution.py:17
  47.3 3.2 collective-permute-start.13
  52.6 59.5 %all-to-all-start = ((f32[2,1,4,256]{2,0,1,3:T(2,128)}), f32[2,1,4,256]{2,0,1,3:T(2,128)S(1)}, u32[]{:S(2)}, u32[]{:S(2)}) async-start(f32[2,1,4,256]{2,0,1,3:T(2,128)} %copy.948), calls=%async_computation | async-start | bytes 524288 | tf_op jit(solution)/shard_map/all_to_all | solution.py:159
  65.1 40.9 %copy-start.10 = (f32[4,1,128]{2,1,0:T(1,128)S(1)}, f32[4,1,128]{2,1,0:T(1,128)}, u32[]{:S(2)}) copy-start(f32[4,1,128]{2,1,0:T(1,128)} %param.45) | copy-start | bytes 6148
  107.8 25.7 %collective-permute-start.18 = (f32[2,1,4,12,256]{4,2,3,1,0:T(4,128)S(1)}, f32[2,1,4,12,256]{4,2,3,1,0:T(4,128)S(1)}, u32[]{:S(2)}, u32[]{:S(2)}) collective-permute-start(f32[2,1,4,12,256]{4,2,3,1,0:T(4,128)S(1)} %fusion.1104), channel_id=1, source_target_pairs={{1,0},{2,1},{3,2},{4,3},{5,4},{6,5},{7,6},{8,7},{9,8},{10,9},{11,1... | collective-permute-start | bytes 294920 | tf_op jit(solution)/shard_map/ppermute | solution.py:18
  109.1 24.4 %collective-permute-start.19 = (f32[2,1,4,12,256]{4,2,3,1,0:T(4,128)S(1)}, f32[2,1,4,12,256]{4,2,3,1,0:T(4,128)S(1)}, u32[]{:S(2)}, u32[]{:S(2)}) collective-permute-start(f32[2,1,4,12,256]{4,2,3,1,0:T(4,128)S(1)} %fusion.1104), channel_id=1, source_target_pairs={{0,1},{1,2},{2,3},{3,4},{4,5},{5,6},{6,7},{7,8},{8,9},{9,10},{10,1... | collective-permute-start | bytes 294920 | tf_op jit(solution)/shard_map/ppermute | solution.py:17
  113.6 14.4 %all-to-all-start.3 = ((f32[2,1,128,8]{3,0,1,2:T(2,128)}), f32[2,1,128,8]{3,0,1,2:T(2,128)S(1)}, u32[]{:S(2)}, u32[]{:S(2)}) async-start(f32[2,1,128,8]{3,0,1,2:T(2,128)} %copy.978), calls=%async_computation.3 | async-start | bytes 262144 | tf_op jit(solution)/shard_map/all_to_all | solution.py:131
  119.9 8.4 %collective-permute-start.7 = (f32[3,2,1,4,4,128]{5,4,3,2,1,0:T(4,128)S(1)}, f32[3,2,1,4,4,128]{5,4,3,2,1,0:T(4,128)S(1)}, u32[]{:S(2)}, u32[]{:S(2)}) collective-permute-start(f32[3,2,1,4,4,128]{5,4,3,2,1,0:T(4,128)S(1)} %get-tuple-element.243), channel_id=1, source_target_pairs={{1,0},{2,1},{3,2},{4,3},{5,4},{6,5},{7,6},{8,7},{9,8},{10,9},{11,1... | collective-permute-start | bytes 147464 | tf_op jit(solution)/shard_map/ppermute | solution.py:18
  121.2 7.2 %collective-permute-start.6 = (f32[3,2,1,4,4,128]{5,4,3,2,1,0:T(4,128)S(1)}, f32[3,2,1,4,4,128]{5,4,3,2,1,0:T(4,128)S(1)}, u32[]{:S(2)}, u32[]{:S(2)}) collective-permute-start(f32[3,2,1,4,4,128]{5,4,3,2,1,0:T(4,128)S(1)} %get-tuple-element.242), channel_id=1, source_target_pairs={{0,1},{1,2},{2,3},{3,4},{4,5},{5,6},{6,7},{7,8},{8,9},{9,10},{10,1... | collective-permute-start | bytes 147464 | tf_op jit(solution)/shard_map/ppermute | solution.py:17
  129.1 9.5 %collective-permute-start.9 = (f32[3,2,1,4,4,128]{5,4,3,2,1,0:T(4,128)S(1)}, f32[3,2,1,4,4,128]{5,4,3,2,1,0:T(4,128)S(1)}, u32[]{:S(2)}, u32[]{:S(2)}) collective-permute-start(f32[3,2,1,4,4,128]{5,4,3,2,1,0:T(4,128)S(1)} %get-tuple-element.241), channel_id=1, source_target_pairs={{1,0},{2,1},{3,2},{4,3},{5,4},{6,5},{7,6},{8,7},{9,8},{10,9},{11,1... | collective-permute-start | bytes 147464 | tf_op jit(solution)/shard_map/ppermute | solution.py:18
  130.4 8.2 %collective-permute-start.8 = (f32[3,2,1,4,4,128]{5,4,3,2,1,0:T(4,128)S(1)}, f32[3,2,1,4,4,128]{5,4,3,2,1,0:T(4,128)S(1)}, u32[]{:S(2)}, u32[]{:S(2)}) collective-permute-start(f32[3,2,1,4,4,128]{5,4,3,2,1,0:T(4,128)S(1)} %get-tuple-element.240), channel_id=1, source_target_pairs={{0,1},{1,2},{2,3},{3,4},{4,5},{5,6},{6,7},{7,8},{8,9},{9,10},{10,1... | collective-permute-start | bytes 147464 | tf_op jit(solution)/shard_map/ppermute | solution.py:17
  133.9 5.2 %collective-permute-start.20 = (f32[2,1,4,12,256]{4,2,3,1,0:T(4,128)S(1)}, f32[2,1,4,12,256]{4,2,3,1,0:T(4,128)S(1)}, u32[]{:S(2)}, u32[]{:S(2)}) collective-permute-start(f32[2,1,4,12,256]{4,2,3,1,0:T(4,128)S(1)} %get-tuple-element.220), channel_id=1, source_target_pairs={{0,1},{1,2},{2,3},{3,4},{4,5},{5,6},{6,7},{7,8},{8,9},{9,10},{10,1... | collective-permute-start | bytes 294920 | tf_op jit(solution)/shard_map/ppermute | solution.py:17
  137.3 3.2 collective-permute-start.21
  142.7 59.0 %all-to-all-start.2 = ((f32[2,1,4,256]{2,0,1,3:T(2,128)}), f32[2,1,4,256]{2,0,1,3:T(2,128)S(1)}, u32[]{:S(2)}, u32[]{:S(2)}) async-start(f32[2,1,4,256]{2,0,1,3:T(2,128)} %copy.966), calls=%async_computation.2 | async-start | bytes 524288 | tf_op jit(solution)/shard_map/all_to_all | solution.py:159
  197.3 25.7 %collective-permute-start.24 = (f32[2,1,4,12,256]{4,2,3,1,0:T(4,128)S(1)}, f32[2,1,4,12,256]{4,2,3,1,0:T(4,128)S(1)}, u32[]{:S(2)}, u32[]{:S(2)}) collective-permute-start(f32[2,1,4,12,256]{4,2,3,1,0:T(4,128)S(1)} %fusion.1105), channel_id=1, source_target_pairs={{1,0},{2,1},{3,2},{4,3},{5,4},{6,5},{7,6},{8,7},{9,8},{10,9},{11,1... | collective-permute-start | bytes 294920 | tf_op jit(solution)/shard_map/ppermute | solution.py:18
  198.6 24.4 %collective-permute-start.25 = (f32[2,1,4,12,256]{4,2,3,1,0:T(4,128)S(1)}, f32[2,1,4,12,256]{4,2,3,1,0:T(4,128)S(1)}, u32[]{:S(2)}, u32[]{:S(2)}) collective-permute-start(f32[2,1,4,12,256]{4,2,3,1,0:T(4,128)S(1)} %fusion.1105), channel_id=1, source_target_pairs={{0,1},{1,2},{2,3},{3,4},{4,5},{5,6},{6,7},{7,8},{8,9},{9,10},{10,1... | collective-permute-start | bytes 294920 | tf_op jit(solution)/shard_map/ppermute | solution.py:17
  203.1 14.4 %all-to-all-start.5 = ((f32[2,1,128,8]{3,0,1,2:T(2,128)}), f32[2,1,128,8]{3,0,1,2:T(2,128)S(1)}, u32[]{:S(2)}, u32[]{:S(2)}) async-start(f32[2,1,128,8]{3,0,1,2:T(2,128)} %copy.989), calls=%async_computation.5 | async-start | bytes 262144 | tf_op jit(solution)/shard_map/all_to_all | solution.py:131
  209.4 8.4 %collective-permute-start.15 = (f32[3,2,1,4,4,128]{5,4,3,2,1,0:T(4,128)S(1)}, f32[3,2,1,4,4,128]{5,4,3,2,1,0:T(4,128)S(1)}, u32[]{:S(2)}, u32[]{:S(2)}) collective-permute-start(f32[3,2,1,4,4,128]{5,4,3,2,1,0:T(4,128)S(1)} %get-tuple-element.239), channel_id=1, source_target_pairs={{1,0},{2,1},{3,2},{4,3},{5,4},{6,5},{7,6},{8,7},{9,8},{10,9},{11,1... | collective-permute-start | bytes 147464 | tf_op jit(solution)/shard_map/ppermute | solution.py:18
  210.7 7.2 %collective-permute-start.14 = (f32[3,2,1,4,4,128]{5,4,3,2,1,0:T(4,128)S(1)}, f32[3,2,1,4,4,128]{5,4,3,2,1,0:T(4,128)S(1)}, u32[]{:S(2)}, u32[]{:S(2)}) collective-permute-start(f32[3,2,1,4,4,128]{5,4,3,2,1,0:T(4,128)S(1)} %get-tuple-element.238), channel_id=1, source_target_pairs={{0,1},{1,2},{2,3},{3,4},{4,5},{5,6},{6,7},{7,8},{8,9},{9,10},{10,1... | collective-permute-start | bytes 147464 | tf_op jit(solution)/shard_map/ppermute | solution.py:17
  218.6 9.5 %collective-permute-start.17 = (f32[3,2,1,4,4,128]{5,4,3,2,1,0:T(4,128)S(1)}, f32[3,2,1,4,4,128]{5,4,3,2,1,0:T(4,128)S(1)}, u32[]{:S(2)}, u32[]{:S(2)}) collective-permute-start(f32[3,2,1,4,4,128]{5,4,3,2,1,0:T(4,128)S(1)} %get-tuple-element.237), channel_id=1, source_target_pairs={{1,0},{2,1},{3,2},{4,3},{5,4},{6,5},{7,6},{8,7},{9,8},{10,9},{11,1... | collective-permute-start | bytes 147464 | tf_op jit(solution)/shard_map/ppermute | solution.py:18
  219.9 8.2 %collective-permute-start.16 = (f32[3,2,1,4,4,128]{5,4,3,2,1,0:T(4,128)S(1)}, f32[3,2,1,4,4,128]{5,4,3,2,1,0:T(4,128)S(1)}, u32[]{:S(2)}, u32[]{:S(2)}) collective-permute-start(f32[3,2,1,4,4,128]{5,4,3,2,1,0:T(4,128)S(1)} %get-tuple-element.236), channel_id=1, source_target_pairs={{0,1},{1,2},{2,3},{3,4},{4,5},{5,6},{6,7},{7,8},{8,9},{9,10},{10,1... | collective-permute-start | bytes 147464 | tf_op jit(solution)/shard_map/ppermute | solution.py:17
  223.4 5.2 %collective-permute-start.26 = (f32[2,1,4,12,256]{4,2,3,1,0:T(4,128)S(1)}, f32[2,1,4,12,256]{4,2,3,1,0:T(4,128)S(1)}, u32[]{:S(2)}, u32[]{:S(2)}) collective-permute-start(f32[2,1,4,12,256]{4,2,3,1,0:T(4,128)S(1)} %get-tuple-element.212), channel_id=1, source_target_pairs={{0,1},{1,2},{2,3},{3,4},{4,5},{5,6},{6,7},{7,8},{8,9},{9,10},{10,1... | collective-permute-start | bytes 294920 | tf_op jit(solution)/shard_map/ppermute | solution.py:17
  226.8 3.2 collective-permute-start.27
  232.2 59.0 %all-to-all-start.4 = ((f32[2,1,4,256]{2,0,1,3:T(2,128)}), f32[2,1,4,256]{2,0,1,3:T(2,128)S(1)}, u32[]{:S(2)}, u32[]{:S(2)}) async-start(f32[2,1,4,256]{2,0,1,3:T(2,128)} %copy.981), calls=%async_computation.4 | async-start | bytes 524288 | tf_op jit(solution)/shard_map/all_to_all | solution.py:159
  286.8 21.9 %collective-permute-start.28 = (f32[2,1,4,12,256]{4,2,3,1,0:T(4,128)S(1)}, f32[2,1,4,12,256]{4,2,3,1,0:T(4,128)S(1)}, u32[]{:S(2)}, u32[]{:S(2)}) collective-permute-start(f32[2,1,4,12,256]{4,2,3,1,0:T(4,128)S(1)} %fusion.1106), channel_id=1, source_target_pairs={{1,0},{2,1},{3,2},{4,3},{5,4},{6,5},{7,6},{8,7},{9,8},{10,9},{11,1... | collective-permute-start | bytes 294920 | tf_op jit(solution)/shard_map/ppermute | solution.py:18
  288.1 20.6 %collective-permute-start.29 = (f32[2,1,4,12,256]{4,2,3,1,0:T(4,128)S(1)}, f32[2,1,4,12,256]{4,2,3,1,0:T(4,128)S(1)}, u32[]{:S(2)}, u32[]{:S(2)}) collective-permute-start(f32[2,1,4,12,256]{4,2,3,1,0:T(4,128)S(1)} %fusion.1106), channel_id=1, source_target_pairs={{0,1},{1,2},{2,3},{3,4},{4,5},{5,6},{6,7},{7,8},{8,9},{9,10},{10,1... | collective-permute-start | bytes 294920 | tf_op jit(solution)/shard_map/ppermute | solution.py:17
  292.6 14.4 %all-to-all-start.6 = ((f32[2,1,128,8]{3,0,1,2:T(2,128)}), f32[2,1,128,8]{3,0,1,2:T(2,128)S(1)}, u32[]{:S(2)}, u32[]{:S(2)}) async-start(f32[2,1,128,8]{3,0,1,2:T(2,128)} %copy.992), calls=%async_computation.6 | async-start | bytes 262144 | tf_op jit(solution)/shard_map/all_to_all | solution.py:131
  298.9 8.4 %collective-permute-start.23 = (f32[3,2,1,4,4,128]{5,4,3,2,1,0:T(4,128)S(1)}, f32[3,2,1,4,4,128]{5,4,3,2,1,0:T(4,128)S(1)}, u32[]{:S(2)}, u32[]{:S(2)}) collective-permute-start(f32[3,2,1,4,4,128]{5,4,3,2,1,0:T(4,128)S(1)} %get-tuple-element.235), channel_id=1, source_target_pairs={{1,0},{2,1},{3,2},{4,3},{5,4},{6,5},{7,6},{8,7},{9,8},{10,9},{11,1... | collective-permute-start | bytes 147464 | tf_op jit(solution)/shard_map/ppermute | solution.py:18
  300.2 7.2 %collective-permute-start.22 = (f32[3,2,1,4,4,128]{5,4,3,2,1,0:T(4,128)S(1)}, f32[3,2,1,4,4,128]{5,4,3,2,1,0:T(4,128)S(1)}, u32[]{:S(2)}, u32[]{:S(2)}) collective-permute-start(f32[3,2,1,4,4,128]{5,4,3,2,1,0:T(4,128)S(1)} %get-tuple-element.234), channel_id=1, source_target_pairs={{0,1},{1,2},{2,3},{3,4},{4,5},{5,6},{6,7},{7,8},{8,9},{9,10},{10,1... | collective-permute-start | bytes 147464 | tf_op jit(solution)/shard_map/ppermute | solution.py:17
  309.1 4.1 %collective-permute-start.30 = (f32[2,1,4,12,256]{4,2,3,1,0:T(4,128)S(1)}, f32[2,1,4,12,256]{4,2,3,1,0:T(4,128)S(1)}, u32[]{:S(2)}, u32[]{:S(2)}) collective-permute-start(f32[2,1,4,12,256]{4,2,3,1,0:T(4,128)S(1)} %get-tuple-element.204), channel_id=1, source_target_pairs={{0,1},{1,2},{2,3},{3,4},{4,5},{5,6},{6,7},{7,8},{8,9},{9,10},{10,1... | collective-permute-start | bytes 294920 | tf_op jit(solution)/shard_map/ppermute | solution.py:17
  311.2 3.9 %collective-permute-start.31 = (f32[2,1,4,12,256]{4,2,3,1,0:T(4,128)S(1)}, f32[2,1,4,12,256]{4,2,3,1,0:T(4,128)S(1)}, u32[]{:S(2)}, u32[]{:S(2)}) collective-permute-start(f32[2,1,4,12,256]{4,2,3,1,0:T(4,128)S(1)} %get-tuple-element.204), channel_id=1, source_target_pairs={{1,0},{2,1},{3,2},{4,3},{5,4},{6,5},{7,6},{8,7},{9,8},{10,9},{11,1... | collective-permute-start | bytes 294920 | tf_op jit(solution)/shard_map/ppermute | solution.py:18
  (2 other events, 1.3 us)
where the time goes:
time: 369 us; the launch traced here: 367 us
  blocking collectives  168 us (46%)
  starting transfers between devices  136 us (37%)
  waiting for transfers between devices  21 us (6%)
  other arithmetic  18.8 us (5%)
  local copies, waits for them, and re-layouts  14.5 us (4%)
  between operations  5.44 us (1%)
    psum x4, blocking collectives, on_device(): recorded = lax.psum(partial_record, 'gx')  168 us
    ppermute x16, starting transfers between devices, with_halo(): before = lax.ppermute(last, axis, up)  50.7 us
    all_to_all x3, starting transfers between devices, on_device(): lax.all_to_all(floor_pressure, 'gx', split_axis=3, concat_axis=2, tiled=T...  36.3 us
    all_to_all x4, starting transfers between devices, on_device(): lax.all_to_all(jnp.transpose(vel_z[:, :, :, 0, :], (0, 1, 3, 2)), 'gx', s...  28.3 us
    ppermute x16, starting transfers between devices, with_halo(): after = lax.ppermute(first, axis, down)  20.8 us
    all_to_all x4, waiting for transfers between devices, on_device(): lax.all_to_all(jnp.transpose(vel_z[:, :, :, 0, :], (0, 1, 3, 2)), 'gx', s...  14.8 us
  transfers between devices with their start and end apart: 39, of which 8 were waited for; matrix products, arithmetic and copies ran while one was open for 5% of the time, Pallas kernels for 0%

commit v1 on v0

--- a/solution.py
+++ b/solution.py
@@ -128,12 +128,20 @@
         vel_z = vel_z + TIME_STEP * solid_buoy * (
             stencil(stress_pad[2], 2, False) + derive(sig_yz, 4, False) + derive(sig_zz, 3, True)
         )
-        floor_velocity = lax.all_to_all(
-            jnp.transpose(vel_z[:, :, :, 0, :], (0, 1, 3, 2)),
-            "gx",
-            split_axis=2,
-            concat_axis=3,
-            tiled=True,
+        floor_velocity = jnp.concatenate(
+            lax.all_to_all(
+                jnp.stack(
+                    jnp.split(
+                        jnp.transpose(vel_z[:, :, :, 0, :], (0, 1, 3, 2)),
+                        lax.axis_size("gx"),
+                        axis=2,
+                    )
+                ),
+                "gx",
+                0,
+                0,
+            ),
+            axis=3,
         )
         flow_x = (flow_x - TIME_STEP * water_buoy * water_derive(pressure, 4, True)) * live
         flow_y = (flow_y - TIME_STEP * water_buoy * water_derive(pressure, 2, True)) * live

time: 369 us -> 456 us (1.24)
  local copies, waits for them, and re-layouts: 14.5 us -> 101 us
    unnamed x34 -> x161, local copies, waits for them, and re-layouts: 4.22 us -> 79.2 us
    split x0 -> x136, local copies, waits for them, and re-layouts: none -> 11.6 us  [on_device(): jnp.split(jnp.transpose(vel_z[:, :, :, 0, :], (0, 1, 3, 2)), lax.axis_siz...]
    all_to_all x3, starting transfers between devices: 36.3 us -> 31.2 us  [on_device(): lax.all_to_all(floor_pressure, 'gx', split_axis=3, concat_axis=2, tiled=T...]
  transfers between devices with their start and end apart: 39 -> 39, of which waited for: 8 -> 8; matrix products, arithmetic and copies ran while one was open for 5% -> 23% of each run, Pallas kernels for 0% -> 0%
where the time goes in v1:
time: 456 us; the launch traced here: 453 us
  blocking collectives  168 us (37%)
  starting transfers between devices  134 us (29%)
  local copies, waits for them, and re-layouts  101 us (22%)
  waiting for transfers between devices  25.2 us (6%)
  other arithmetic  15.9 us (3%)
  between operations  5.63 us (1%)
    psum x4, blocking collectives, on_device(): recorded = lax.psum(partial_record, 'gx')  168 us
    unnamed x161, local copies, waits for them, and re-layouts  79.2 us
    ppermute x16, starting transfers between devices, with_halo(): before = lax.ppermute(last, axis, up)  52.3 us
    all_to_all x3, starting transfers between devices, on_device(): lax.all_to_all(floor_pressure, 'gx', split_axis=3, concat_axis=2, tiled=T...  31.2 us
    all_to_all x4, starting transfers between devices, on_device(): lax.all_to_all(jnp.stack(jnp.split(jnp.transpose(vel_z[:, :, :, 0, :], (0...  29.9 us
    ppermute x16, starting transfers between devices, with_halo(): after = lax.ppermute(first, axis, down)  20.8 us
    all_to_all x4, waiting for transfers between devices, on_device(): lax.all_to_all(jnp.stack(jnp.split(jnp.transpose(vel_z[:, :, :, 0, :], (0...  19.1 us
    split x136, local copies, waits for them, and re-layouts, on_device(): jnp.split(jnp.transpose(vel_z[:, :, :, 0, :], (0, 1, 3, 2)), lax.axis_siz...  11.6 us
  transfers between devices with their start and end apart: 39, of which 8 were waited for; matrix products, arithmetic and copies ran while one was open for 23% of the time, Pallas kernels for 0%

profile of v1, /device:TPU:0, one launch (start us, length us, event | category | flops | bytes accessed | tf_op | source)
XLA Modules:
  0.0 453.2 jit_solution(6304260693991118387)
XLA Ops:
  2.8 3.0 collective-permute-start.11
  7.7 1.3 collective-permute-start.1
  9.0 5.1 %collective-permute-start = (f32[3,2,1,4,4,128]{5,3,4,1,2,0:T(4,128)S(1)}, f32[3,2,1,4,4,128]{5,3,4,1,2,0:T(4,128)S(1)}, u32[]{:S(2)}, u32[]{:S(2)}) collective-permute-start(f32[3,2,1,4,4,128]{5,3,4,1,2,0:T(4,128)S(1)} %get-tuple-element.240), channel_id=1, source_target_pairs={{0,1},{1,2},{2,3},{3,4},{4,5},{5,6},{6,7},{7,8},{8,9},{9,10},{10,1... | collective-permute-start | bytes 147464 | tf_op jit(solution)/shard_map/ppermute | solution.py:17
  42.1 9.7 %all-to-all-start.1 = ((f32[32,2,1,4,8]{4,3,2,1,0:T(4,128)}), f32[32,2,1,4,8]{4,3,2,1,0:T(4,128)S(1)}, u32[]{:S(2)}, u32[]{:S(2)}) async-start(f32[32,2,1,4,8]{4,3,2,1,0:T(4,128)} %bitcast.268), calls=%async_computation.1 | async-start | bytes 262144 | tf_op jit(solution)/shard_map/all_to_all | solution.py:132
  52.2 1.4 collective-permute-start.3
  53.6 3.0 collective-permute-start.2
  56.7 3.4 all-to-all-done.1
  60.9 1.3 collective-permute-start.5
  62.2 3.0 collective-permute-start.4
  65.8 3.4 collective-permute-start.12
  69.1 1.3 collective-permute-start.13
  70.8 1.5 collective-permute-done.13
  74.5 12.3 %all-to-all-start = ((f32[2,1,4,256]{2,0,1,3:T(2,128)}), f32[2,1,4,256]{2,0,1,3:T(2,128)S(1)}, u32[]{:S(2)}, u32[]{:S(2)}) async-start(f32[2,1,4,256]{2,0,1,3:T(2,128)} %copy.2757), calls=%async_computation | async-start | bytes 524288 | tf_op jit(solution)/shard_map/all_to_all | solution.py:167
  87.3 40.5 %psum.28 = f32[1,128]{1,0:T(1,128)S(1)} all-reduce(f32[1,128]{1,0:T(1,128)S(1)} %fusion.7), channel_id=1, replica_groups=mesh['groups'=1,'gx'=32] {'gx'}, use_global_device_ids=true, to_apply=%region_2.3 | all-reduce | flops 128 | bytes 1024 | tf_op jit(solution)/shard_map/psum | solution.py:197
  129.5 1.3 collective-permute-start.18
  130.8 3.0 collective-permute-start.19
  156.4 6.2 %all-to-all-start.3 = ((f32[32,2,1,4,8]{4,3,2,1,0:T(4,128)}), f32[32,2,1,4,8]{4,3,2,1,0:T(4,128)S(1)}, u32[]{:S(2)}, u32[]{:S(2)}) async-start(f32[32,2,1,4,8]{4,3,2,1,0:T(4,128)} %bitcast.413), calls=%async_computation.3 | async-start | bytes 262144 | tf_op jit(solution)/shard_map/all_to_all | solution.py:132
  162.6 1.3 collective-permute-start.7
  163.9 3.0 collective-permute-start.6
  167.0 3.8 all-to-all-done.3
  171.6 1.3 collective-permute-start.9
  172.9 3.0 collective-permute-start.8
  176.4 3.4 collective-permute-start.20
  179.8 1.3 collective-permute-start.21
  181.5 1.5 collective-permute-done.21
  185.2 11.9 %all-to-all-start.2 = ((f32[2,1,4,256]{2,0,1,3:T(2,128)}), f32[2,1,4,256]{2,0,1,3:T(2,128)S(1)}, u32[]{:S(2)}, u32[]{:S(2)}) async-start(f32[2,1,4,256]{2,0,1,3:T(2,128)} %copy.2873), calls=%async_computation.2 | async-start | bytes 524288 | tf_op jit(solution)/shard_map/all_to_all | solution.py:167
  197.6 40.5 %psum.29 = f32[1,128]{1,0:T(1,128)S(1)} all-reduce(f32[1,128]{1,0:T(1,128)S(1)} %fusion.5), channel_id=1, replica_groups=mesh['groups'=1,'gx'=32] {'gx'}, use_global_device_ids=true, to_apply=%region_6.7 | all-reduce | flops 128 | bytes 1024 | tf_op jit(solution)/shard_map/psum | solution.py:197
  239.8 1.3 collective-permute-start.24
  241.1 3.2 collective-permute-start.25
  245.2 1.3 collective-permute-start.15
  246.5 4.4 collective-permute-start.14
  272.6 7.8 %all-to-all-start.5 = ((f32[32,2,1,4,8]{4,3,2,1,0:T(4,128)}), f32[32,2,1,4,8]{4,3,2,1,0:T(4,128)S(1)}, u32[]{:S(2)}, u32[]{:S(2)}) async-start(f32[32,2,1,4,8]{4,3,2,1,0:T(4,128)} %bitcast.503), calls=%async_computation.5 | async-start | bytes 262144 | tf_op jit(solution)/shard_map/all_to_all | solution.py:132
  280.6 8.1 %all-to-all-done.5 = f32[32,2,1,4,8]{4,3,2,1,0:T(4,128)S(1)} async-done(((f32[32,2,1,4,8]{4,3,2,1,0:T(4,128)}), f32[32,2,1,4,8]{4,3,2,1,0:T(4,128)S(1)}, u32[]{:S(2)}, u32[]{:S(2)}) %all-to-all-start.5) | async-done | bytes 8224 | tf_op jit(solution)/shard_map/all_to_all | solution.py:132
  289.4 1.3 collective-permute-start.17
  290.7 3.0 collective-permute-start.16
  294.3 3.4 collective-permute-start.26
  297.6 1.3 collective-permute-start.27
  299.3 1.5 collective-permute-done.27
  303.0 7.0 %all-to-all-start.4 = ((f32[2,1,4,256]{2,0,1,3:T(2,128)}), f32[2,1,4,256]{2,0,1,3:T(2,128)S(1)}, u32[]{:S(2)}, u32[]{:S(2)}) async-start(f32[2,1,4,256]{2,0,1,3:T(2,128)} %copy.2993), calls=%async_computation.4 | async-start | bytes 524288 | tf_op jit(solution)/shard_map/all_to_all | solution.py:167
  310.5 40.5 %psum.30 = f32[1,128]{1,0:T(1,128)S(1)} all-reduce(f32[1,128]{1,0:T(1,128)S(1)} %fusion.3), channel_id=1, replica_groups=mesh['groups'=1,'gx'=32] {'gx'}, use_global_device_ids=true, to_apply=%region_10.11 | all-reduce | flops 128 | bytes 1024 | tf_op jit(solution)/shard_map/psum | solution.py:197
  354.0 3.0 collective-permute-start.29
  379.6 6.2 %all-to-all-start.6 = ((f32[32,2,1,4,8]{4,3,2,1,0:T(4,128)}), f32[32,2,1,4,8]{4,3,2,1,0:T(4,128)S(1)}, u32[]{:S(2)}, u32[]{:S(2)}) async-start(f32[32,2,1,4,8]{4,3,2,1,0:T(4,128)} %bitcast.546), calls=%async_computation.6 | async-start | bytes 262144 | tf_op jit(solution)/shard_map/all_to_all | solution.py:132
  387.2 3.0 collective-permute-start.22
  390.3 3.8 all-to-all-done.6
  395.2 2.1 collective-permute-start.30
  399.9 1.4 collective-permute-done.31
  403.1 46.5 %psum.31 = f32[1,128]{1,0:T(1,128)S(1)} all-reduce(f32[1,128]{1,0:T(1,128)S(1)} %fusion.1), channel_id=1, replica_groups=mesh['groups'=1,'gx'=32] {'gx'}, use_global_device_ids=true, to_apply=%region_13.14 | all-reduce | flops 128 | bytes 1024 | tf_op jit(solution)/shard_map/psum | solution.py:197
  451.3 1.4 fusion.371
  (494 shorter events, 124.2 us)
Async XLA Ops:
  1.5 63.7 %collective-permute-start.10 = (f32[2,1,4,12,256]{4,2,3,1,0:T(4,128)S(1)}, f32[2,1,4,12,256]{4,2,3,1,0:T(4,128)S(1)}, u32[]{:S(2)}, u32[]{:S(2)}) collective-permute-start(f32[2,1,4,12,256]{4,2,3,1,0:T(4,128)S(1)} %slice_bitcast_fusion.3), channel_id=1, source_target_pairs={{1,0},{2,1},{3,2},{4,3},{5,4},{6,5},{7,6},{8,7},{9,8},{10,9},{11,1... | collective-permute-start | bytes 294920 | tf_op jit(solution)/shard_map/ppermute | solution.py:18
  2.8 62.5 %collective-permute-start.11 = (f32[2,1,4,12,256]{4,2,3,1,0:T(4,128)S(1)}, f32[2,1,4,12,256]{4,2,3,1,0:T(4,128)S(1)}, u32[]{:S(2)}, u32[]{:S(2)}) collective-permute-start(f32[2,1,4,12,256]{4,2,3,1,0:T(4,128)S(1)} %slice_bitcast_fusion.3), channel_id=1, source_target_pairs={{0,1},{1,2},{2,3},{3,4},{4,5},{5,6},{6,7},{7,8},{8,9},{9,10},{10,1... | collective-permute-start | bytes 294920 | tf_op jit(solution)/shard_map/ppermute | solution.py:17
  6.8 0.8 slice-start
  7.6 6.4 %copy-start.6 = (s32[4,256]{1,0:T(4,128)S(1)}, s32[4,256]{1,0:T(4,128)}, u32[]{:S(2)}) copy-start(s32[4,256]{1,0:T(4,128)} %param.41) | copy-start | bytes 12292
  7.7 12.3 %collective-permute-start.1 = (f32[3,2,1,4,4,128]{5,3,4,1,2,0:T(4,128)S(1)}, f32[3,2,1,4,4,128]{5,3,4,1,2,0:T(4,128)S(1)}, u32[]{:S(2)}, u32[]{:S(2)}) collective-permute-start(f32[3,2,1,4,4,128]{5,3,4,1,2,0:T(4,128)S(1)} %get-tuple-element.241), channel_id=1, source_target_pairs={{1,0},{2,1},{3,2},{4,3},{5,4},{6,5},{7,6},{8,7},{9,8},{10,9},{11,1... | collective-permute-start | bytes 147464 | tf_op jit(solution)/shard_map/ppermute | solution.py:18
  9.0 11.0 %collective-permute-start = (f32[3,2,1,4,4,128]{5,3,4,1,2,0:T(4,128)S(1)}, f32[3,2,1,4,4,128]{5,3,4,1,2,0:T(4,128)S(1)}, u32[]{:S(2)}, u32[]{:S(2)}) collective-permute-start(f32[3,2,1,4,4,128]{5,3,4,1,2,0:T(4,128)S(1)} %get-tuple-element.240), channel_id=1, source_target_pairs={{0,1},{1,2},{2,3},{3,4},{4,5},{5,6},{6,7},{7,8},{8,9},{9,10},{10,1... | collective-permute-start | bytes 147464 | tf_op jit(solution)/shard_map/ppermute | solution.py:17
  14.1 0.7 copy-start.3
  14.8 0.7 copy-start.4
  15.5 0.8 copy-start.1
  16.3 0.8 copy-start.2
  18.6 0.7 copy-start.5
  42.1 18.0 %all-to-all-start.1 = ((f32[32,2,1,4,8]{4,3,2,1,0:T(4,128)}), f32[32,2,1,4,8]{4,3,2,1,0:T(4,128)S(1)}, u32[]{:S(2)}, u32[]{:S(2)}) async-start(f32[32,2,1,4,8]{4,3,2,1,0:T(4,128)} %bitcast.268), calls=%async_computation.1 | async-start | bytes 262144 | tf_op jit(solution)/shard_map/all_to_all | solution.py:132
  52.2 8.1 %copy-start = (f32[4,2,1,4,12,256]{5,3,4,2,1,0:T(4,128)S(1)}, f32[4,2,1,4,12,256]{5,3,4,2,1,0:T(4,128)}, u32[]{:S(2)}) copy-start(f32[4,2,1,4,12,256]{5,3,4,2,1,0:T(4,128)} %param.35) | copy-start | bytes 1179652
  52.2 8.2 %collective-permute-start.3 = (f32[3,2,1,4,4,128]{5,3,4,1,2,0:T(4,128)S(1)}, f32[3,2,1,4,4,128]{5,3,4,1,2,0:T(4,128)S(1)}, u32[]{:S(2)}, u32[]{:S(2)}) collective-permute-start(f32[3,2,1,4,4,128]{5,3,4,1,2,0:T(4,128)S(1)} %get-tuple-element.239), channel_id=1, source_target_pairs={{1,0},{2,1},{3,2},{4,3},{5,4},{6,5},{7,6},{8,7},{9,8},{10,9},{11,1... | collective-permute-start | bytes 147464 | tf_op jit(solution)/shard_map/ppermute | solution.py:18
  53.6 6.8 %collective-permute-start.2 = (f32[3,2,1,4,4,128]{5,3,4,1,2,0:T(4,128)S(1)}, f32[3,2,1,4,4,128]{5,3,4,1,2,0:T(4,128)S(1)}, u32[]{:S(2)}, u32[]{:S(2)}) collective-permute-start(f32[3,2,1,4,4,128]{5,3,4,1,2,0:T(4,128)S(1)} %get-tuple-element.238), channel_id=1, source_target_pairs={{0,1},{1,2},{2,3},{3,4},{4,5},{5,6},{6,7},{7,8},{8,9},{9,10},{10,1... | collective-permute-start | bytes 147464 | tf_op jit(solution)/shard_map/ppermute | solution.py:17
  60.9 9.5 %collective-permute-start.5 = (f32[3,2,1,4,4,128]{5,3,4,1,2,0:T(4,128)S(1)}, f32[3,2,1,4,4,128]{5,3,4,1,2,0:T(4,128)S(1)}, u32[]{:S(2)}, u32[]{:S(2)}) collective-permute-start(f32[3,2,1,4,4,128]{5,3,4,1,2,0:T(4,128)S(1)} %get-tuple-element.237), channel_id=1, source_target_pairs={{1,0},{2,1},{3,2},{4,3},{5,4},{6,5},{7,6},{8,7},{9,8},{10,9},{11,1... | collective-permute-start | bytes 147464 | tf_op jit(solution)/shard_map/ppermute | solution.py:18
  62.2 8.2 %collective-permute-start.4 = (f32[3,2,1,4,4,128]{5,3,4,1,2,0:T(4,128)S(1)}, f32[3,2,1,4,4,128]{5,3,4,1,2,0:T(4,128)S(1)}, u32[]{:S(2)}, u32[]{:S(2)}) collective-permute-start(f32[3,2,1,4,4,128]{5,3,4,1,2,0:T(4,128)S(1)} %get-tuple-element.236), channel_id=1, source_target_pairs={{0,1},{1,2},{2,3},{3,4},{4,5},{5,6},{6,7},{7,8},{8,9},{9,10},{10,1... | collective-permute-start | bytes 147464 | tf_op jit(solution)/shard_map/ppermute | solution.py:17
  65.8 5.0 %collective-permute-start.12 = (f32[2,1,4,12,256]{4,2,3,1,0:T(4,128)S(1)}, f32[2,1,4,12,256]{4,2,3,1,0:T(4,128)S(1)}, u32[]{:S(2)}, u32[]{:S(2)}) collective-permute-start(f32[2,1,4,12,256]{4,2,3,1,0:T(4,128)S(1)} %get-tuple-element.186), channel_id=1, source_target_pairs={{0,1},{1,2},{2,3},{3,4},{4,5},{5,6},{6,7},{7,8},{8,9},{9,10},{10,1... | collective-permute-start | bytes 294920 | tf_op jit(solution)/shard_map/ppermute | solution.py:17
  69.1 3.2 collective-permute-start.13
  74.5 59.4 %all-to-all-start = ((f32[2,1,4,256]{2,0,1,3:T(2,128)}), f32[2,1,4,256]{2,0,1,3:T(2,128)S(1)}, u32[]{:S(2)}, u32[]{:S(2)}) async-start(f32[2,1,4,256]{2,0,1,3:T(2,128)} %copy.2757), calls=%async_computation | async-start | bytes 524288 | tf_op jit(solution)/shard_map/all_to_all | solution.py:167
  86.9 40.9 %copy-start.9 = (f32[4,1,128]{2,1,0:T(1,128)S(1)}, f32[4,1,128]{2,1,0:T(1,128)}, u32[]{:S(2)}) copy-start(f32[4,1,128]{2,1,0:T(1,128)} %param.45) | copy-start | bytes 6148
  129.5 46.4 %collective-permute-start.18 = (f32[2,1,4,12,256]{4,2,3,1,0:T(4,128)S(1)}, f32[2,1,4,12,256]{4,2,3,1,0:T(4,128)S(1)}, u32[]{:S(2)}, u32[]{:S(2)}) collective-permute-start(f32[2,1,4,12,256]{4,2,3,1,0:T(4,128)S(1)} %fusion.861), channel_id=1, source_target_pairs={{1,0},{2,1},{3,2},{4,3},{5,4},{6,5},{7,6},{8,7},{9,8},{10,9},{11,1... | collective-permute-start | bytes 294920 | tf_op jit(solution)/shard_map/ppermute | solution.py:18
  130.8 45.1 %collective-permute-start.19 = (f32[2,1,4,12,256]{4,2,3,1,0:T(4,128)S(1)}, f32[2,1,4,12,256]{4,2,3,1,0:T(4,128)S(1)}, u32[]{:S(2)}, u32[]{:S(2)}) collective-permute-start(f32[2,1,4,12,256]{4,2,3,1,0:T(4,128)S(1)} %fusion.861), channel_id=1, source_target_pairs={{0,1},{1,2},{2,3},{3,4},{4,5},{5,6},{6,7},{7,8},{8,9},{9,10},{10,1... | collective-permute-start | bytes 294920 | tf_op jit(solution)/shard_map/ppermute | solution.py:17
  156.4 14.4 %all-to-all-start.3 = ((f32[32,2,1,4,8]{4,3,2,1,0:T(4,128)}), f32[32,2,1,4,8]{4,3,2,1,0:T(4,128)S(1)}, u32[]{:S(2)}, u32[]{:S(2)}) async-start(f32[32,2,1,4,8]{4,3,2,1,0:T(4,128)} %bitcast.413), calls=%async_computation.3 | async-start | bytes 262144 | tf_op jit(solution)/shard_map/all_to_all | solution.py:132
  162.6 8.4 %collective-permute-start.7 = (f32[3,2,1,4,4,128]{5,3,4,1,2,0:T(4,128)S(1)}, f32[3,2,1,4,4,128]{5,3,4,1,2,0:T(4,128)S(1)}, u32[]{:S(2)}, u32[]{:S(2)}) collective-permute-start(f32[3,2,1,4,4,128]{5,3,4,1,2,0:T(4,128)S(1)} %get-tuple-element.235), channel_id=1, source_target_pairs={{1,0},{2,1},{3,2},{4,3},{5,4},{6,5},{7,6},{8,7},{9,8},{10,9},{11,1... | collective-permute-start | bytes 147464 | tf_op jit(solution)/shard_map/ppermute | solution.py:18
  163.9 7.2 %collective-permute-start.6 = (f32[3,2,1,4,4,128]{5,3,4,1,2,0:T(4,128)S(1)}, f32[3,2,1,4,4,128]{5,3,4,1,2,0:T(4,128)S(1)}, u32[]{:S(2)}, u32[]{:S(2)}) collective-permute-start(f32[3,2,1,4,4,128]{5,3,4,1,2,0:T(4,128)S(1)} %get-tuple-element.234), channel_id=1, source_target_pairs={{0,1},{1,2},{2,3},{3,4},{4,5},{5,6},{6,7},{7,8},{8,9},{9,10},{10,1... | collective-permute-start | bytes 147464 | tf_op jit(solution)/shard_map/ppermute | solution.py:17
  171.6 9.5 %collective-permute-start.9 = (f32[3,2,1,4,4,128]{5,3,4,1,2,0:T(4,128)S(1)}, f32[3,2,1,4,4,128]{5,3,4,1,2,0:T(4,128)S(1)}, u32[]{:S(2)}, u32[]{:S(2)}) collective-permute-start(f32[3,2,1,4,4,128]{5,3,4,1,2,0:T(4,128)S(1)} %get-tuple-element.233), channel_id=1, source_target_pairs={{1,0},{2,1},{3,2},{4,3},{5,4},{6,5},{7,6},{8,7},{9,8},{10,9},{11,1... | collective-permute-start | bytes 147464 | tf_op jit(solution)/shard_map/ppermute | solution.py:18
  172.9 8.2 %collective-permute-start.8 = (f32[3,2,1,4,4,128]{5,3,4,1,2,0:T(4,128)S(1)}, f32[3,2,1,4,4,128]{5,3,4,1,2,0:T(4,128)S(1)}, u32[]{:S(2)}, u32[]{:S(2)}) collective-permute-start(f32[3,2,1,4,4,128]{5,3,4,1,2,0:T(4,128)S(1)} %get-tuple-element.232), channel_id=1, source_target_pairs={{0,1},{1,2},{2,3},{3,4},{4,5},{5,6},{6,7},{7,8},{8,9},{9,10},{10,1... | collective-permute-start | bytes 147464 | tf_op jit(solution)/shard_map/ppermute | solution.py:17
  176.4 5.0 %collective-permute-start.20 = (f32[2,1,4,12,256]{4,2,3,1,0:T(4,128)S(1)}, f32[2,1,4,12,256]{4,2,3,1,0:T(4,128)S(1)}, u32[]{:S(2)}, u32[]{:S(2)}) collective-permute-start(f32[2,1,4,12,256]{4,2,3,1,0:T(4,128)S(1)} %get-tuple-element.213), channel_id=1, source_target_pairs={{0,1},{1,2},{2,3},{3,4},{4,5},{5,6},{6,7},{7,8},{8,9},{9,10},{10,1... | collective-permute-start | bytes 294920 | tf_op jit(solution)/shard_map/ppermute | solution.py:17
  179.8 3.2 collective-permute-start.21
  185.2 59.1 %all-to-all-start.2 = ((f32[2,1,4,256]{2,0,1,3:T(2,128)}), f32[2,1,4,256]{2,0,1,3:T(2,128)S(1)}, u32[]{:S(2)}, u32[]{:S(2)}) async-start(f32[2,1,4,256]{2,0,1,3:T(2,128)} %copy.2873), calls=%async_computation.2 | async-start | bytes 524288 | tf_op jit(solution)/shard_map/all_to_all | solution.py:167
  239.8 54.0 %collective-permute-start.24 = (f32[2,1,4,12,256]{4,2,3,1,0:T(4,128)S(1)}, f32[2,1,4,12,256]{4,2,3,1,0:T(4,128)S(1)}, u32[]{:S(2)}, u32[]{:S(2)}) collective-permute-start(f32[2,1,4,12,256]{4,2,3,1,0:T(4,128)S(1)} %fusion.862), channel_id=1, source_target_pairs={{1,0},{2,1},{3,2},{4,3},{5,4},{6,5},{7,6},{8,7},{9,8},{10,9},{11,1... | collective-permute-start | bytes 294920 | tf_op jit(solution)/shard_map/ppermute | solution.py:18
  241.1 52.7 %collective-permute-start.25 = (f32[2,1,4,12,256]{4,2,3,1,0:T(4,128)S(1)}, f32[2,1,4,12,256]{4,2,3,1,0:T(4,128)S(1)}, u32[]{:S(2)}, u32[]{:S(2)}) collective-permute-start(f32[2,1,4,12,256]{4,2,3,1,0:T(4,128)S(1)} %fusion.862), channel_id=1, source_target_pairs={{0,1},{1,2},{2,3},{3,4},{4,5},{5,6},{6,7},{7,8},{8,9},{9,10},{10,1... | collective-permute-start | bytes 294920 | tf_op jit(solution)/shard_map/ppermute | solution.py:17
  245.2 43.8 %collective-permute-start.15 = (f32[3,2,1,4,4,128]{5,3,4,1,2,0:T(4,128)S(1)}, f32[3,2,1,4,4,128]{5,3,4,1,2,0:T(4,128)S(1)}, u32[]{:S(2)}, u32[]{:S(2)}) collective-permute-start(f32[3,2,1,4,4,128]{5,3,4,1,2,0:T(4,128)S(1)} %get-tuple-element.231), channel_id=1, source_target_pairs={{1,0},{2,1},{3,2},{4,3},{5,4},{6,5},{7,6},{8,7},{9,8},{10,9},{11,1... | collective-permute-start | bytes 147464 | tf_op jit(solution)/shard_map/ppermute | solution.py:18
  246.5 42.5 %collective-permute-start.14 = (f32[3,2,1,4,4,128]{5,3,4,1,2,0:T(4,128)S(1)}, f32[3,2,1,4,4,128]{5,3,4,1,2,0:T(4,128)S(1)}, u32[]{:S(2)}, u32[]{:S(2)}) collective-permute-start(f32[3,2,1,4,4,128]{5,3,4,1,2,0:T(4,128)S(1)} %get-tuple-element.230), channel_id=1, source_target_pairs={{0,1},{1,2},{2,3},{3,4},{4,5},{5,6},{6,7},{7,8},{8,9},{9,10},{10,1... | collective-permute-start | bytes 147464 | tf_op jit(solution)/shard_map/ppermute | solution.py:17
  272.6 16.1 %all-to-all-start.5 = ((f32[32,2,1,4,8]{4,3,2,1,0:T(4,128)}), f32[32,2,1,4,8]{4,3,2,1,0:T(4,128)S(1)}, u32[]{:S(2)}, u32[]{:S(2)}) async-start(f32[32,2,1,4,8]{4,3,2,1,0:T(4,128)} %bitcast.503), calls=%async_computation.5 | async-start | bytes 262144 | tf_op jit(solution)/shard_map/all_to_all | solution.py:132
  289.4 9.5 %collective-permute-start.17 = (f32[3,2,1,4,4,128]{5,3,4,1,2,0:T(4,128)S(1)}, f32[3,2,1,4,4,128]{5,3,4,1,2,0:T(4,128)S(1)}, u32[]{:S(2)}, u32[]{:S(2)}) collective-permute-start(f32[3,2,1,4,4,128]{5,3,4,1,2,0:T(4,128)S(1)} %get-tuple-element.229), channel_id=1, source_target_pairs={{1,0},{2,1},{3,2},{4,3},{5,4},{6,5},{7,6},{8,7},{9,8},{10,9},{11,1... | collective-permute-start | bytes 147464 | tf_op jit(solution)/shard_map/ppermute | solution.py:18
  290.7 8.2 %collective-permute-start.16 = (f32[3,2,1,4,4,128]{5,3,4,1,2,0:T(4,128)S(1)}, f32[3,2,1,4,4,128]{5,3,4,1,2,0:T(4,128)S(1)}, u32[]{:S(2)}, u32[]{:S(2)}) collective-permute-start(f32[3,2,1,4,4,128]{5,3,4,1,2,0:T(4,128)S(1)} %get-tuple-element.228), channel_id=1, source_target_pairs={{0,1},{1,2},{2,3},{3,4},{4,5},{5,6},{6,7},{7,8},{8,9},{9,10},{10,1... | collective-permute-start | bytes 147464 | tf_op jit(solution)/shard_map/ppermute | solution.py:17
  294.3 5.0 %collective-permute-start.26 = (f32[2,1,4,12,256]{4,2,3,1,0:T(4,128)S(1)}, f32[2,1,4,12,256]{4,2,3,1,0:T(4,128)S(1)}, u32[]{:S(2)}, u32[]{:S(2)}) collective-permute-start(f32[2,1,4,12,256]{4,2,3,1,0:T(4,128)S(1)} %get-tuple-element.205), channel_id=1, source_target_pairs={{0,1},{1,2},{2,3},{3,4},{4,5},{5,6},{6,7},{7,8},{8,9},{9,10},{10,1... | collective-permute-start | bytes 294920 | tf_op jit(solution)/shard_map/ppermute | solution.py:17
  297.6 3.2 collective-permute-start.27
  303.0 54.0 %all-to-all-start.4 = ((f32[2,1,4,256]{2,0,1,3:T(2,128)}), f32[2,1,4,256]{2,0,1,3:T(2,128)S(1)}, u32[]{:S(2)}, u32[]{:S(2)}) async-start(f32[2,1,4,256]{2,0,1,3:T(2,128)} %copy.2993), calls=%async_computation.4 | async-start | bytes 524288 | tf_op jit(solution)/shard_map/all_to_all | solution.py:167
  352.7 42.0 %collective-permute-start.28 = (f32[2,1,4,12,256]{4,2,3,1,0:T(4,128)S(1)}, f32[2,1,4,12,256]{4,2,3,1,0:T(4,128)S(1)}, u32[]{:S(2)}, u32[]{:S(2)}) collective-permute-start(f32[2,1,4,12,256]{4,2,3,1,0:T(4,128)S(1)} %fusion.863), channel_id=1, source_target_pairs={{1,0},{2,1},{3,2},{4,3},{5,4},{6,5},{7,6},{8,7},{9,8},{10,9},{11,1... | collective-permute-start | bytes 294920 | tf_op jit(solution)/shard_map/ppermute | solution.py:18
  354.0 40.7 %collective-permute-start.29 = (f32[2,1,4,12,256]{4,2,3,1,0:T(4,128)S(1)}, f32[2,1,4,12,256]{4,2,3,1,0:T(4,128)S(1)}, u32[]{:S(2)}, u32[]{:S(2)}) collective-permute-start(f32[2,1,4,12,256]{4,2,3,1,0:T(4,128)S(1)} %fusion.863), channel_id=1, source_target_pairs={{0,1},{1,2},{2,3},{3,4},{4,5},{5,6},{6,7},{7,8},{8,9},{9,10},{10,1... | collective-permute-start | bytes 294920 | tf_op jit(solution)/shard_map/ppermute | solution.py:17
  379.6 14.4 %all-to-all-start.6 = ((f32[32,2,1,4,8]{4,3,2,1,0:T(4,128)}), f32[32,2,1,4,8]{4,3,2,1,0:T(4,128)S(1)}, u32[]{:S(2)}, u32[]{:S(2)}) async-start(f32[32,2,1,4,8]{4,3,2,1,0:T(4,128)} %bitcast.546), calls=%async_computation.6 | async-start | bytes 262144 | tf_op jit(solution)/shard_map/all_to_all | solution.py:132
  385.9 8.4 %collective-permute-start.23 = (f32[3,2,1,4,4,128]{5,3,4,1,2,0:T(4,128)S(1)}, f32[3,2,1,4,4,128]{5,3,4,1,2,0:T(4,128)S(1)}, u32[]{:S(2)}, u32[]{:S(2)}) collective-permute-start(f32[3,2,1,4,4,128]{5,3,4,1,2,0:T(4,128)S(1)} %get-tuple-element.227), channel_id=1, source_target_pairs={{1,0},{2,1},{3,2},{4,3},{5,4},{6,5},{7,6},{8,7},{9,8},{10,9},{11,1... | collective-permute-start | bytes 147464 | tf_op jit(solution)/shard_map/ppermute | solution.py:18
  387.2 7.1 %collective-permute-start.22 = (f32[3,2,1,4,4,128]{5,3,4,1,2,0:T(4,128)S(1)}, f32[3,2,1,4,4,128]{5,3,4,1,2,0:T(4,128)S(1)}, u32[]{:S(2)}, u32[]{:S(2)}) collective-permute-start(f32[3,2,1,4,4,128]{5,3,4,1,2,0:T(4,128)S(1)} %get-tuple-element.226), channel_id=1, source_target_pairs={{0,1},{1,2},{2,3},{3,4},{4,5},{5,6},{6,7},{7,8},{8,9},{9,10},{10,1... | collective-permute-start | bytes 147464 | tf_op jit(solution)/shard_map/ppermute | solution.py:17
  395.2 4.7 %collective-permute-start.30 = (f32[2,1,4,12,256]{4,2,3,1,0:T(4,128)S(1)}, f32[2,1,4,12,256]{4,2,3,1,0:T(4,128)S(1)}, u32[]{:S(2)}, u32[]{:S(2)}) collective-permute-start(f32[2,1,4,12,256]{4,2,3,1,0:T(4,128)S(1)} %get-tuple-element.197), channel_id=1, source_target_pairs={{0,1},{1,2},{2,3},{3,4},{4,5},{5,6},{6,7},{7,8},{8,9},{9,10},{10,1... | collective-permute-start | bytes 294920 | tf_op jit(solution)/shard_map/ppermute | solution.py:17
  397.4 3.9 collective-permute-start.31
  (2 other events, 1.3 us)
